TPU v7x, 128 devices: a whole 4x4x4 slice. The times are simulated.
128 devices in a mesh: seq: 32 (over x, y, core), wa: 4 (over z).
Axes of the slice: x: 4, y: 4, z: 4, core: 2. Of those that a mesh axis runs over, the one named last changes fastest.
Arguments:
- hidden_in: bfloat16 [16384, 2048], P('seq', 'wa'), may hold values from -6 to 6
- request_spans: int32 [4, 2], replicated, may hold values from 0 to 16384, as said below
- owners: int32 [4], replicated, may hold values from 0 to 31, as said below
- mixer_gain: float32 [2048], replicated, may hold values from 0.1 to 1.9
- query_weight: bfloat16 [2048, 2048], P(None, 'wa'), may hold values from -0.125 to 0.125
- forget_weight: bfloat16 [2048, 2048], P(None, 'wa'), may hold values from -0.0625 to 0.0625
- input_weight: bfloat16 [2048, 2048], P(None, 'wa'), may hold values from -0.125 to 0.125
- gate_weight: bfloat16 [2048, 2048], P(None, 'wa'), may hold values from -0.125 to 0.125
- forget_bias: float32 [2048], P('wa')
- output_weight: bfloat16 [2048, 2048], P('wa'), may hold values from -0.125 to 0.125
- swiglu_gain: float32 [2048], replicated, may hold values from 0.1 to 1.9
- swiglu_gate: bfloat16 [2048, 3072], P(None, 'wa'), may hold values from -0.125 to 0.125
- swiglu_up: bfloat16 [2048, 3072], P(None, 'wa'), may hold values from -0.125 to 0.125
- swiglu_down: bfloat16 [3072, 2048], P('wa'), may hold values from -0.109375 to 0.109375
Outputs:
- hidden_out: bfloat16 [16384, 2048], P('seq', 'wa')
- handed_state: float32 [32, 16, 128, 128], P('seq', 'wa')
Inputs may be any that keep to these rules, and one draw needn't show every extreme that they name: Requests lie back to back in order: request_spans[0, 0] = 0, each request's end equals the next one's start, the last end is 16384, and every request holds at least 64 tokens. The owners are distinct indices along seq; the last request's owner is the index half of 32 minus one; the first request's owner is the index just before that of the device holding the first request's last token, counted round; the index 31 is always an owner.
All inputs are finite; a program needn't handle non-finite values.
Results may differ from a plain program's by a relative error of at most 0.009.
Values may be sent and summed in bfloat16 or wider, within the bound.
No kernel may reach another device: no remote copies, remote signals or barrier semaphores. Data moves between devices by JAX's collectives and lax.ppermute only.
A program may use at most 128 MiB of HBM per device.

v0:
```python
import jax
import jax.numpy as jnp
from jax import lax
from jax.sharding import PartitionSpec as P

HEAD = 128
GROUP = 64
REQS = 4


EPS = 1e-06
HIGH = lax.Precision.HIGHEST


def entering(value, axis, join, neutral):
    count, mine = (lax.axis_size(axis), lax.axis_index(axis))
    pieces = jax.tree.map(lambda part: lax.all_gather(part, axis), value)
    so_far = jax.tree.map(
        lambda part, zero: jnp.full_like(part, 0) + jnp.asarray(zero, part.dtype), value, neutral
    )

    def hop(position, so_far):
        longer = join(so_far, jax.tree.map(lambda part: part[position], pieces))
        return jax.tree.map(lambda new, old: jnp.where(position < mine, new, old), longer, so_far)

    return lax.fori_loop(0, count - 1, hop, so_far)


def rms_rows(matrix, scaling):
    matrix = matrix.astype(jnp.float32)
    rescale = lax.rsqrt(jnp.mean(matrix * matrix, axis=-1, keepdims=True) + EPS)
    return (matrix * rescale * scaling).astype(jnp.bfloat16)


def project(matrix, weight):
    return jnp.dot(matrix, weight, preferred_element_type=jnp.float32)


def widen_rows(shard_part):
    return lax.all_gather(shard_part, "wa", axis=1, tiled=True)


def narrow_sum(partial_terms):
    return lax.psum_scatter(partial_terms, "wa", scatter_dimension=1, tiled=True)


def local(
    hidden_in,
    request_spans,
    owners,
    mixer_gain,
    query_weight,
    forget_weight,
    input_weight,
    gate_weight,
    forget_bias,
    output_weight,
    swiglu_gain,
    swiglu_gate,
    swiglu_up,
    swiglu_down,
):
    tok_rows = hidden_in.shape[0]
    head_count = query_weight.shape[1] // HEAD
    block_count = tok_rows // GROUP
    gathered = widen_rows(hidden_in)
    normed = rms_rows(gathered, mixer_gain)
    queries = jax.nn.silu(project(normed, query_weight))
    forget_logit = project(normed, forget_weight) + forget_bias
    log_decay = jax.nn.log_sigmoid(forget_logit)
    key_rows = jax.nn.sigmoid(-forget_logit)
    value_rows = project(normed, input_weight)
    gate_logit = project(normed, gate_weight)
    first_row = lax.axis_index("seq") * tok_rows
    position = first_row + jnp.arange(tok_rows, dtype=jnp.int32)
    start_rows = request_spans[:, 0]
    end_rows = request_spans[:, 1]
    is_start = jnp.any(position[:, None] == start_rows[None, :], axis=1)
    segment = jnp.sum((start_rows[None, :] <= position[:, None]).astype(jnp.int32), axis=1) - 1
    shape_four = (block_count, GROUP, head_count, HEAD)
    query_parts = queries.reshape(shape_four)
    key_parts = key_rows.reshape(shape_four)
    value_parts = value_rows.reshape(shape_four)
    segment_parts = segment.reshape(block_count, GROUP)
    keep_mask = (1.0 - is_start.astype(jnp.float32)).reshape(block_count, GROUP)
    cum_decay = jnp.cumsum(log_decay.reshape(shape_four), axis=1)
    surviving = jnp.cumprod(keep_mask, axis=1)
    query_tilde = query_parts * jnp.exp(cum_decay)
    key_tilde = key_parts * jnp.exp(-cum_decay)
    offsets = jnp.arange(GROUP, dtype=jnp.int32)
    causal = offsets[:, None] >= offsets[None, :]
    same_doc = causal[None] & (segment_parts[:, :, None] == segment_parts[:, None, :])
    scores = jnp.einsum("nihc,njhc->nhij", query_tilde, key_tilde, precision=HIGH)
    scores = jnp.where(same_doc[:, None], scores, 0.0)
    inner_out = jnp.einsum("nhij,njhd->nihd", scores, value_parts, precision=HIGH)
    tail_mask = (segment_parts == segment_parts[:, -1:]).astype(jnp.float32)
    last_decay = jnp.exp(cum_decay[:, -1])
    fresh = last_decay[..., None] * jnp.einsum(
        "njhc,njhd->nhcd", key_tilde * tail_mask[:, :, None, None], value_parts, precision=HIGH
    )
    shrink = surviving[:, -1][:, None, None] * last_decay

    def advance(carried, blocked):
        running, product = carried
        shrink_part, fresh_part = blocked
        return (
            (shrink_part[..., None] * running + fresh_part, product * shrink_part),
            (running, product),
        )

    initial = (
        jnp.zeros((head_count, HEAD, HEAD), jnp.float32),
        jnp.ones((head_count, HEAD), jnp.float32),
    )
    (local_state, device_decay), (start_state, start_decay) = lax.scan(
        advance, initial, (shrink, fresh)
    )

    def combine(earlier, follower):
        return (earlier[0] * follower[0], follower[0][..., None] * earlier[1] + follower[1])

    identity = (jnp.ones_like(device_decay), jnp.zeros_like(local_state))
    incoming = entering((device_decay, local_state), "seq", combine, identity)[1]
    block_state = start_state + start_decay[..., None] * incoming[None]
    carried_out = jnp.einsum("nihc,nhcd->nihd", query_tilde, block_state, precision=HIGH)
    mixer_out = (inner_out + surviving[:, :, None, None] * carried_out).reshape(
        tok_rows, head_count, HEAD
    )
    rescale = lax.rsqrt(jnp.mean(mixer_out * mixer_out, axis=-1, keepdims=True) + EPS)
    gate_heads = jax.nn.silu(gate_logit.reshape(tok_rows, head_count, HEAD))
    mixed_rows = (
        (mixer_out * rescale * gate_heads).reshape(tok_rows, head_count * HEAD).astype(jnp.bfloat16)
    )
    collected = []
    for request in range(REQS):
        local_end = end_rows[request] - 1 - first_row
        inside = (local_end >= 0) & (local_end < tok_rows)
        end_row = jnp.clip(local_end, 0, tok_rows - 1)
        block_index = end_row // GROUP
        within = end_row % GROUP
        decay_block = lax.dynamic_index_in_dim(cum_decay, block_index, 0, keepdims=False)
        key_block = lax.dynamic_index_in_dim(key_tilde, block_index, 0, keepdims=False)
        value_block = lax.dynamic_index_in_dim(value_parts, block_index, 0, keepdims=False)
        segment_block = lax.dynamic_index_in_dim(segment_parts, block_index, 0, keepdims=False)
        alive_block = lax.dynamic_index_in_dim(surviving, block_index, 0, keepdims=False)
        state_block = lax.dynamic_index_in_dim(block_state, block_index, 0, keepdims=False)
        decay_end = lax.dynamic_index_in_dim(decay_block, within, 0, keepdims=False)
        segment_end = lax.dynamic_index_in_dim(segment_block, within, 0, keepdims=False)
        alive_end = lax.dynamic_index_in_dim(alive_block, within, 0, keepdims=False)
        upto_mask = ((offsets <= within) & (segment_block == segment_end)).astype(jnp.float32)
        partial_end = jnp.einsum(
            "jhc,jhd->hcd", key_block * upto_mask[:, None, None], value_block, precision=HIGH
        )
        end_state = jnp.exp(decay_end)[..., None] * (alive_end * state_block + partial_end)
        collected.append(jnp.where(inside, end_state, 0.0))
    end_states = jnp.stack(collected)
    summed_states = lax.psum(end_states.astype(jnp.bfloat16), "seq").astype(jnp.float32)
    owned_mask = (owners == lax.axis_index("seq")).astype(jnp.float32)
    handed_state = jnp.einsum("r,rhcd->hcd", owned_mask, summed_states, precision=HIGH)[None]
    partial_terms = project(mixed_rows, output_weight)
    residual = (hidden_in.astype(jnp.float32) + narrow_sum(partial_terms)).astype(jnp.bfloat16)
    widened = widen_rows(residual)
    normed_ffn = rms_rows(widened, swiglu_gain)
    hidden = (
        jax.nn.silu(project(normed_ffn, swiglu_gate)) * project(normed_ffn, swiglu_up)
    ).astype(jnp.bfloat16)
    hidden_out = (residual.astype(jnp.float32) + narrow_sum(project(hidden, swiglu_down))).astype(
        jnp.bfloat16
    )
    return (hidden_out, handed_state)


def solution(mesh):
    in_specs = (
        P("seq", "wa"),
        P(),
        P(),
        P(),
        P(None, "wa"),
        P(None, "wa"),
        P(None, "wa"),
        P(None, "wa"),
        P("wa"),
        P("wa", None),
        P(),
        P(None, "wa"),
        P(None, "wa"),
        P("wa", None),
    )
    out_specs = (P("seq", "wa"), P("seq", "wa", None, None))
    return jax.shard_map(local, mesh=mesh, in_specs=in_specs, out_specs=out_specs, check_vma=False)
```

profile of v0, /device:TPU:0, one launch (start us, length us, event | category | flops | bytes accessed | tf_op | source)
XLA Modules:
  0.0 450.6 jit_solution(12406958529448473247)
XLA Ops:
  9.9 33.3 %all-gather.7.cloned.1.call-done = bf16[512,2048]{1,0:T(8,128)(2,1)} async-done(((bf16[512,512]{1,0:T(8,128)(2,1)}), bf16[512,2048]{1,0:T(8,128)(2,1)}) %all-gather.7.cloned.1.call-update) | async-done | bytes 2097168 | tf_op jit(solution)/shard_map/all_gather | solution.py:40
  45.5 4.9 %add_divide_fusion = (f32[512,512]{1,0:T(8,128)}, f32[512,512]{1,0:T(8,128)}) fusion(f32[512]{0:T(512)S(1)} %copy-done.15, bf16[2048,512]{1,0:T(8,128)(2,1)} %param.23, bf16[512,2048]{1,0:T(8,128)(2,1)S(1)} %copy-done.8, f32[2048]{0:T(1024)S(1)} %copy-done.13, f32[512]{0:T(512)S(1)} %add_rsqrt_fusion.1), kind=kOutput, calls=%fused_computation.60 | convolution fusion | flops 1080819712 | bytes 6303744 | tf_op jit(solution)/shard_map/dot_general | solution.py:36
  50.4 2.5 reshape.259
  52.9 2.6 reshape.260
  55.5 4.7 %divide_multiply_fusion = f32[512,512]{1,0:T(8,128)} fusion(bf16[2048,512]{1,0:T(8,128)(2,1)} %param.22, bf16[512,2048]{1,0:T(8,128)(2,1)} %all-gather.7.cloned.1.call-done, f32[2048]{0:T(1024)S(1)} %copy-done.13, f32[512]{0:T(512)S(1)} %add_rsqrt_fusion.1), kind=kOutput, calls=%fused_computation.61 | convolution fusion | flops 1078984704 | bytes 5253120 | tf_op jit(solution)/shard_map/dot_general | solution.py:36
  60.2 2.5 reshape.258
  62.8 4.9 %broadcast_multiply_fusion = (f32[8,64,4,128]{3,0,1,2:T(8,128)}, f32[8,64,4,128]{3,0,1,2:T(8,128)}, f32[8,64,4,128]{3,0,1,2:T(8,128)}, f32[8,64,4,128]{3,0,1,2:T(8,128)S(1)}) fusion(f32[8,64]{0,1:T(8,128)S(1)} %copy.108, f32[8,64,4,128]{3,2,1,0:T(4,128)} %reshape.260, f32[8,64,4,128]{3,2,1,0:T(4,128)} %reshape.258, f32[8,64,4,128]{3,2,1,0:T(4,128)} %reshape.259), kind=kOutput, calls=%fused_computation.70 | output fusion | flops 17563648 | bytes 7342080 | tf_op jit(solution)/shard_map/jit(cumsum)/reduce_window_sum | solution.py:86
  70.9 2.5 reshape.257
  74.2 6.8 %convolution_multiply_fusion = f32[8,4,128,128]{3,2,1,0:T(8,128)} fusion(f32[8,64,4,128]{3,0,1,2:T(8,128)} %get-tuple-element.249, f32[8,4,128]{2,1,0:T(4,128)S(1)} %copy.107, f32[8,64,4,128]{3,2,1,0:T(4,128)} %reshape.257), kind=kOutput, calls=%fused_computation.20 | convolution fusion | flops 403177472 | bytes 4210688 | tf_op jit(solution)/shard_map/njhc,njhd->nhcd/dot_general | solution.py:98
  81.0 15.2 %while.31 = (s32[]{:T(128)}, f32[4,128,128]{2,1,0:T(8,128)S(1)}, f32[4,128]{1,0:T(4,128)S(1)}, f32[8,4,128,128]{3,2,1,0:T(8,128)}, f32[8,4,128]{2,1,0:T(4,128)S(...) while((s32[]{:T(128)}, f32[4,128,128]{2,1,0:T(8,128)S(1)}, ...), condition=%wide.region_6.7_spmd.clone, body=%wide.region_5.6_spmd.clone.sunk | while | flops 263683 | bytes 1327734 | solution.py:115
  97.2 24.2 %all-gather.2 = f32[32,4,128]{2,1,0:T(4,128)S(1)} all-gather(f32[1,4,128]{2,1,0:T(4,128)S(1)} %bitcast.142), channel_id=2, replica_groups=mesh['seq'=32,'wa'=4] {'seq'}, dimensions={0}, use_global_device_ids=true | all-gather | bytes 67584 | tf_op jit(solution)/shard_map/all_gather | solution.py:17
  121.4 4.5 %convolution_select_fusion = f32[8,4,64,64]{3,2,1,0:T(8,128)} fusion(f32[8,64,4,128]{3,0,1,2:T(8,128)} %get-tuple-element.250, f32[8,64,4,128]{3,0,1,2:T(8,128)} %get-tuple-element.263, pred[8,64,64]{2,1,0:T(8,128)(4,1)S(1)} %compare_and_fusion), kind=kOutput, calls=%fused_computation.25 | convolution fusion | flops 201457664 | bytes 2654208 | tf_op jit(solution)/shard_map/nihc,njhc->nhij/dot_general | solution.py:93
  125.9 23.9 %all-gather.11.cloned.1.call-done = f32[128,128,128]{2,1,0:T(8,128)} async-done(((f32[4,128,128]{2,1,0:T(8,128)}), f32[128,128,128]{2,1,0:T(8,128)}) %all-gather.11.cloned.1.call-update) | async-done | bytes 8388624 | tf_op jit(solution)/shard_map/all_gather | solution.py:17
  149.8 37.0 %while.32 = (s32[]{:T(128)}, f32[4,128,128]{2,1,0:T(8,128)S(1)}, s32[]{:T(128)}, f32[32,4,128]{2,1,0:T(4,128)S(1)}, f32[32,4,128,128]{3,2,1,0:T(8,128)}, /*index=5*/s32[]{:T(128)}, s32[]{:T(128)}) while((s32[]{:T(128)}, f32[4,128,128]{2,1,0:T(8,128)S(1)}, s32[]{:T(128)}, f32[32,4,128]{2,1,0:T(4,128)S(1)}, ...), condition=%wide.region_8.9_spmd.clone, body=%wide.region_7.8_spmd.clone.sunk | while | flops 262148 | bytes 792681 | solution.py:26
  193.5 2.9 copy.113
  198.0 8.0 %fusion.40 = f32[512,2048]{1,0:T(8,128)} fusion(bf16[512,2048]{1,0:T(8,128)(2,1)} %param.27, f32[64,8,4,128]{3,2,1,0:T(4,128)} %bitcast.133, f32[64,8,4,128]{3,2,1,0:T(4,128)} %bitcast.135, bf16[2048,512]{1,0:T(8,128)(2,1)} %param.25, bf16[512,2048]{1,0:T(8,128)(2,1)} %all-gather.7.cloned.1.call-done, f32[2048]{0:T(1024)S(1)} %copy-done.13, ...), kind=kOutput, calls=%fused_computation.68 | convolution fusion | flops 2153512960 | bytes 12593152 | tf_op jit(solution)/shard_map/dot_general | solution.py:36
  206.1 46.8 %reduce-scatter.3.cloned.1.call-done = f32[512,512]{1,0:T(8,128)} async-done(((f32[512,2048]{1,0:T(8,128)}), f32[512,512]{1,0:T(8,128)}) %reduce-scatter.3.cloned.1.call-update) | async-done | bytes 1048592 | tf_op jit(solution)/shard_map/reduce_scatter | solution.py:44
  259.9 2.4 fusion.71
  263.2 3.2 constant_dynamic-slice_fusion.15
  273.8 12.2 %all-gather.9.cloned.1.call-done = bf16[512,2048]{1,0:T(8,128)(2,1)} async-done(((bf16[512,512]{1,0:T(8,128)(2,1)}), bf16[512,2048]{1,0:T(8,128)(2,1)}) %all-gather.9.cloned.1.call-update) | async-done | bytes 2097168 | tf_op jit(solution)/shard_map/all_gather | solution.py:40
  288.3 5.0 %fusion.38 = f32[512,768]{1,0:T(8,128)} fusion(bf16[2048,768]{1,0:T(8,128)(2,1)} %param.29, bf16[512,2048]{1,0:T(8,128)(2,1)S(1)} %copy-done.7, f32[2048]{0:T(1024)S(1)} %copy-done.14, f32[512]{0:T(512)S(1)} %add_rsqrt_fusion), kind=kOutput, calls=%fused_computation.67 | convolution fusion | flops 1614807040 | bytes 6825984 | tf_op jit(solution)/shard_map/dot_general | solution.py:36
  293.2 8.9 %fusion.35 = f32[512,2048]{1,0:T(8,128)} fusion(bf16[768,2048]{1,0:T(8,128)(2,1)S(1)} %copy-done, f32[512,768]{1,0:T(8,128)} %fusion.38, bf16[2048,768]{1,0:T(8,128)(2,1)} %param.30, bf16[512,2048]{1,0:T(8,128)(2,1)} %all-gather.9.cloned.1.call-done, f32[2048]{0:T(1024)S(1)} %copy-done.14, f32[512]{0:T(512)S(1)} %add_rsqrt_fusion), kind=kOutput, calls=%fused_computation.66 | convolution fusion | flops 3227779072 | bytes 14166016 | tf_op jit(solution)/shard_map/dot_general | solution.py:36
  302.2 90.5 %all-reduce.2.cloned.1.call-done = bf16[4,4,128,128]{3,2,1,0:T(8,128)(2,1)} async-done(((bf16[4,4,128,128]{3,2,1,0:T(8,128)(2,1)}), bf16[4,4,128,128]{3,2,1,0:T(8,128)(2,1)}) %all-reduce.2.cloned.1.call-update) | async-done | bytes 524304 | tf_op jit(solution)/shard_map/psum | solution.py:157
  394.9 46.5 %reduce-scatter.5.cloned.1.call-done = f32[512,512]{1,0:T(8,128)} async-done(((f32[512,2048]{1,0:T(8,128)}), f32[512,512]{1,0:T(8,128)}) %reduce-scatter.5.cloned.1.call-update) | async-done | bytes 1048592 | tf_op jit(solution)/shard_map/reduce_scatter | solution.py:44
  (195 shorter events, 88.6 us)
Async XLA Ops:
  7.2 286.1 %copy-start = (bf16[768,2048]{1,0:T(8,128)(2,1)S(1)}, bf16[768,2048]{1,0:T(8,128)(2,1)}, u32[]{:S(2)}) copy-start(bf16[768,2048]{1,0:T(8,128)(2,1)} %param.31) | copy-start | bytes 9437188
  7.2 38.3 %copy-start.13 = (f32[2048]{0:T(1024)S(1)}, f32[2048]{0:T(1024)}, u32[]{:S(2)}) copy-start(f32[2048]{0:T(1024)} %param.21) | copy-start | bytes 24580
  7.2 38.3 %copy-start.15 = (f32[512]{0:T(512)S(1)}, f32[512]{0:T(512)}, u32[]{:S(2)}) copy-start(f32[512]{0:T(512)} %param.26) | copy-start | bytes 6148
  7.2 36.1 %all-gather.7.cloned.1.call-start = ((), (), s32[]{:S(2)}) async-start(), calls=%async_computation.2 | async-start | bytes 2621440 | tf_op jit(solution)/shard_map/all_gather | solution.py:40
  7.9 141.9 %all-gather.11.cloned.1.call-start = ((), (), s32[]{:S(2)}) async-start(), calls=%async_computation.7 | async-start | bytes 8650752 | tf_op jit(solution)/shard_map/all_gather | solution.py:17
  43.3 2.3 copy-start.8
  62.8 5.9 %copy-start.9 = (bf16[512,2048]{1,0:T(8,128)(2,1)S(1)}, bf16[512,2048]{1,0:T(8,128)(2,1)}, u32[]{:S(2)}) copy-start(bf16[512,2048]{1,0:T(8,128)(2,1)} %all-gather.7.cloned.1.call-done) | copy-start | bytes 6291460
  62.8 5.9 %copy-start.12 = (bf16[2048,512]{1,0:T(8,128)(2,1)S(1)}, bf16[2048,512]{1,0:T(8,128)(2,1)}, u32[]{:S(2)}) copy-start(bf16[2048,512]{1,0:T(8,128)(2,1)} %param.24) | copy-start | bytes 6291460
  67.6 1.0 copy-start.10
  96.3 0.7 copy-start.1
  97.0 155.9 %reduce-scatter.3.cloned.1.call-start = ((), (), s32[]{:S(2)}) async-start(), calls=%async_computation.3 | async-start | bytes 5242880 | tf_op jit(solution)/shard_map/reduce_scatter | solution.py:44
  186.8 2.1 copy-start.5
  188.8 2.1 copy-start.2
  188.8 2.1 copy-start.4
  188.9 2.3 copy-start.6
  206.1 49.4 %copy-start.11 = (s32[4,2]{0,1:T(2,128)S(1)}, s32[4,2]{0,1:T(2,128)}, u32[]{:S(2)}) copy-start(s32[4,2]{0,1:T(2,128)} %param.19) | copy-start | bytes 100
  206.1 79.9 %all-gather.9.cloned.1.call-start = ((), (), s32[]{:S(2)}) async-start(), calls=%async_computation.4 | async-start | bytes 2621440 | tf_op jit(solution)/shard_map/all_gather | solution.py:40
  255.2 137.4 %all-reduce.2.cloned.1.call-start = ((), (), s32[]{:S(2)}) async-start(), calls=%async_computation.6 | async-start | bytes 1048576 | tf_op jit(solution)/shard_map/psum | solution.py:157
  258.6 8.9 %copy-start.3 = (f32[8,4,128,128]{3,2,1,0:T(8,128)S(1)}, f32[8,4,128,128]{3,2,1,0:T(8,128)}, u32[]{:S(2)}) copy-start(f32[8,4,128,128]{3,2,1,0:T(8,128)} %copy-done.2) | copy-start | bytes 6291460
  271.5 16.8 %copy-start.14 = (f32[2048]{0:T(1024)S(1)}, f32[2048]{0:T(1024)}, u32[]{:S(2)}) copy-start(f32[2048]{0:T(1024)} %param.28) | copy-start | bytes 24580
  273.7 167.7 %reduce-scatter.5.cloned.1.call-start = ((), (), s32[]{:S(2)}) async-start(), calls=%async_computation.5 | async-start | bytes 5242880 | tf_op jit(solution)/shard_map/reduce_scatter | solution.py:44
  286.0 2.2 copy-start.7
  302.2 90.5 %copy-start.16 = (s32[4]{0:T(128)S(1)}, s32[4]{0:T(128)}, u32[]{:S(2)}) copy-start(s32[4]{0:T(128)} %param.20) | copy-start | bytes 52
Sparse Core Ops, SparseCore 0:
  9.7 33.5 all-gather.6
  97.1 52.6 all-gather.10
  206.2 46.6 reduce-scatter.2
  255.3 30.6 all-gather.8
  289.4 103.2 all-reduce.1
  394.9 46.4 reduce-scatter.4
where the time goes:
time: 453 us; the launch traced here: 451 us
  waiting for transfers between devices  254 us (56%)
  other arithmetic  71.2 us (16%)
  matrix products  56.8 us (13%)
  local copies, waits for them, and re-layouts  25.6 us (6%)
  blocking collectives  24.2 us (5%)
  between operations  17 us (4%)
    reduce_scatter x2, waiting for transfers between devices, narrow_sum(): lax.psum_scatter(partial_terms, 'wa', scatter_dimension=1, tiled=True)  93.3 us
    psum x1, waiting for transfers between devices, local(): lax.psum(end_states.astype(jnp.bfloat16), 'seq').astype(jnp.float32)  90.5 us
    all_gather x2, waiting for transfers between devices, widen_rows(): return lax.all_gather(shard_part, 'wa', axis=1, tiled=True)  45.5 us
    select_n x31, other arithmetic, hop(): jnp.where(position < mine, new, old)  35.6 us
    dot_general x6, matrix products, project(): return jnp.dot(matrix, weight, preferred_element_type=jnp.float32)  33.8 us
    all_gather x1, blocking collectives, entering(): pieces = jax.tree.map(lambda part: lax.all_gather(part, axis), value)  24.2 us
    all_gather x1, waiting for transfers between devices, entering(): pieces = jax.tree.map(lambda part: lax.all_gather(part, axis), value)  23.9 us
  transfers between devices with their start and end apart: 6, of which 6 were waited for; matrix products, arithmetic and copies ran while one was open for 9% of the time, Pallas kernels for 0%

commit v1 on v0

--- a/solution.py
+++ b/solution.py
@@ -12,18 +12,44 @@
 HIGH = lax.Precision.HIGHEST
 
 
-def entering(value, axis, join, neutral):
+def entering(decay, state, axis):
     count, mine = (lax.axis_size(axis), lax.axis_index(axis))
-    pieces = jax.tree.map(lambda part: lax.all_gather(part, axis), value)
-    so_far = jax.tree.map(
-        lambda part, zero: jnp.full_like(part, 0) + jnp.asarray(zero, part.dtype), value, neutral
-    )
-
-    def hop(position, so_far):
-        longer = join(so_far, jax.tree.map(lambda part: part[position], pieces))
-        return jax.tree.map(lambda new, old: jnp.where(position < mine, new, old), longer, so_far)
-
-    return lax.fori_loop(0, count - 1, hop, so_far)
+    step_one = [(i, i + 1) for i in range(count - 1)]
+    decay = jnp.where(mine == 0, 1.0, lax.ppermute(decay, axis, step_one))
+    state = lax.ppermute(state, axis, step_one)
+    stride = 1
+    while stride < count:
+        pairs = [(i, i + stride) for i in range(count - stride)]
+        decay_in = lax.ppermute(decay, axis, pairs)
+        state_in = lax.ppermute(state, axis, pairs)
+        has = mine >= stride
+        state = jnp.where(has, decay[..., None] * state_in + state, state)
+        decay = jnp.where(has, decay_in * decay, decay)
+        stride *= 2
+    return state
+
+
+def route_states(end_states, end_rows, owners, tok_rows, axis):
+    count, mine = (lax.axis_size(axis), lax.axis_index(axis))
+    moved = end_states.astype(jnp.bfloat16)
+    left = [(i, (i - 1) % count) for i in range(count)]
+    first = lax.ppermute(moved[0], axis, left)
+    last = lax.ppermute(moved[-1], axis, [(count - 1, count // 2 - 1)])
+    middle = moved[1:-1]
+    place = ((end_rows - 1) // tok_rows)[1:-1]
+    offset = (owners[1:-1] - place) % count
+    for bit in range((count - 1).bit_length()):
+        stride = 1 << bit
+        moving = ((offset >> bit) & 1) == 1
+        go = (moving & (place == mine))[:, None, None, None]
+        sent = jnp.where(go, middle, jnp.zeros_like(middle))
+        got = lax.ppermute(sent, axis, [(i, (i + stride) % count) for i in range(count)])
+        middle = jnp.where(go, jnp.zeros_like(middle), middle) + got
+        place = jnp.where(moving, (place + stride) % count, place)
+    zero = jnp.zeros_like(first)
+    held = jnp.where(owners[0] == mine, first, zero) + jnp.where(owners[-1] == mine, last, zero)
+    held = held + jnp.sum(middle, axis=0)
+    return held.astype(jnp.float32)[None]
 
 
 def rms_rows(matrix, scaling):
@@ -116,11 +142,7 @@
         advance, initial, (shrink, fresh)
     )
 
-    def combine(earlier, follower):
-        return (earlier[0] * follower[0], follower[0][..., None] * earlier[1] + follower[1])
-
-    identity = (jnp.ones_like(device_decay), jnp.zeros_like(local_state))
-    incoming = entering((device_decay, local_state), "seq", combine, identity)[1]
+    incoming = entering(device_decay, local_state, "seq")
     block_state = start_state + start_decay[..., None] * incoming[None]
     carried_out = jnp.einsum("nihc,nhcd->nihd", query_tilde, block_state, precision=HIGH)
     mixer_out = (inner_out + surviving[:, :, None, None] * carried_out).reshape(
@@ -154,9 +176,7 @@
         end_state = jnp.exp(decay_end)[..., None] * (alive_end * state_block + partial_end)
         collected.append(jnp.where(inside, end_state, 0.0))
     end_states = jnp.stack(collected)
-    summed_states = lax.psum(end_states.astype(jnp.bfloat16), "seq").astype(jnp.float32)
-    owned_mask = (owners == lax.axis_index("seq")).astype(jnp.float32)
-    handed_state = jnp.einsum("r,rhcd->hcd", owned_mask, summed_states, precision=HIGH)[None]
+    handed_state = route_states(end_states, end_rows, owners, tok_rows, "seq")
     partial_terms = project(mixed_rows, output_weight)
     residual = (hidden_in.astype(jnp.float32) + narrow_sum(partial_terms)).astype(jnp.bfloat16)
     widened = widen_rows(residual)

time: 453 us -> 360 us (0.79)
  waiting for transfers between devices: 254 us -> 157 us
  starting transfers between devices: 0.46 us -> 52.9 us
  other arithmetic: 71.2 us -> 43.7 us
  blocking collectives: 24.2 us -> 0 us
    psum x1 -> x0, waiting for transfers between devices: 90.5 us -> none  [local(): lax.psum(end_states.astype(jnp.bfloat16), 'seq').astype(jnp.float32)]
    ppermute x0 -> x18, starting transfers between devices: none -> 52.5 us  [the longest x5 33.4 us: entering(): state_in = lax.ppermute(state, axis, pairs)]
    reduce_scatter x2, waiting for transfers between devices: 93.3 us -> 48.6 us  [narrow_sum(): lax.psum_scatter(partial_terms, 'wa', scatter_dimension=1, tiled=True)]
    ppermute x0 -> x18, waiting for transfers between devices: none -> 44.2 us  [the longest x5 40.3 us: route_states(): lax.ppermute(sent, axis, [(i, (i + stride) % count) for i in range(count)])]
    select_n x31 -> x16, other arithmetic: 35.6 us -> 7.54 us  [the longest x5 5.33 us: entering(): state = jnp.where(has, decay[..., None] * state_in + state, state)]
    all_gather x1 -> x0, blocking collectives: 24.2 us -> none  [entering(): pieces = jax.tree.map(lambda part: lax.all_gather(part, axis), value)]
    all_gather x1 -> x0, waiting for transfers between devices: 23.9 us -> none  [entering(): pieces = jax.tree.map(lambda part: lax.all_gather(part, axis), value)]
    all_gather x2, waiting for transfers between devices: 45.5 us -> 63.8 us  [widen_rows(): return lax.all_gather(shard_part, 'wa', axis=1, tiled=True)]
  transfers between devices with their start and end apart: 6 -> 22, of which waited for: 6 -> 14; matrix products, arithmetic and copies ran while one was open for 9% -> 10% of each run, Pallas kernels for 0% -> 0%
where the time goes in v1:
time: 360 us; the launch traced here: 359 us
  waiting for transfers between devices  157 us (44%)
  matrix products  58 us (16%)
  starting transfers between devices  52.9 us (15%)
  other arithmetic  43.7 us (12%)
  local copies, waits for them, and re-layouts  28.2 us (8%)
  between operations  18.3 us (5%)
    all_gather x2, waiting for transfers between devices, widen_rows(): return lax.all_gather(shard_part, 'wa', axis=1, tiled=True)  63.8 us
    reduce_scatter x2, waiting for transfers between devices, narrow_sum(): lax.psum_scatter(partial_terms, 'wa', scatter_dimension=1, tiled=True)  48.6 us
    ppermute x5, waiting for transfers between devices, route_states(): lax.ppermute(sent, axis, [(i, (i + stride) % count) for i in range(count)])  40.3 us
    dot_general x6, matrix products, project(): return jnp.dot(matrix, weight, preferred_element_type=jnp.float32)  34 us
    ppermute x5, starting transfers between devices, entering(): state_in = lax.ppermute(state, axis, pairs)  33.4 us
    ppermute x4, starting transfers between devices, entering(): decay_in = lax.ppermute(decay, axis, pairs)  11.7 us
    dot_general x4, matrix products, local(): jnp.einsum('jhc,jhd->hcd', key_block * upto_mask[:, None, None], value_bl...  9.41 us
    add x8, other arithmetic, advance(): shrink_part[..., None] * running + fresh_part  8.93 us
  transfers between devices with their start and end apart: 22, of which 14 were waited for; matrix products, arithmetic and copies ran while one was open for 10% of the time, Pallas kernels for 0%

profile of v1, /device:TPU:0, one launch (start us, length us, event | category | flops | bytes accessed | tf_op | source)
XLA Modules:
  0.0 358.7 jit_solution(3286885183243488186)
XLA Ops:
  9.9 33.3 %all-gather.3.cloned.1.call-done = bf16[512,2048]{1,0:T(8,128)(2,1)} async-done(((bf16[512,512]{1,0:T(8,128)(2,1)}), bf16[512,2048]{1,0:T(8,128)(2,1)}) %all-gather.3.cloned.1.call-update) | async-done | bytes 2097168 | tf_op jit(solution)/shard_map/all_gather | solution.py:66
  45.5 4.9 %add_divide_fusion = (f32[512,512]{1,0:T(8,128)}, f32[512,512]{1,0:T(8,128)}) fusion(f32[512]{0:T(512)S(1)} %copy-done.14, bf16[2048,512]{1,0:T(8,128)(2,1)} %param.21, bf16[512,2048]{1,0:T(8,128)(2,1)S(1)} %copy-done.4, f32[2048]{0:T(1024)S(1)} %copy-done.12, f32[512]{0:T(512)S(1)} %add_rsqrt_fusion.1), kind=kOutput, calls=%fused_computation.55 | convolution fusion | flops 1080819712 | bytes 6303744 | tf_op jit(solution)/shard_map/dot_general | solution.py:62
  55.5 4.7 %divide_multiply_fusion = f32[512,512]{1,0:T(8,128)} fusion(bf16[2048,512]{1,0:T(8,128)(2,1)} %param.20, bf16[512,2048]{1,0:T(8,128)(2,1)} %all-gather.3.cloned.1.call-done, f32[2048]{0:T(1024)S(1)} %copy-done.12, f32[512]{0:T(512)S(1)} %add_rsqrt_fusion.1), kind=kOutput, calls=%fused_computation.56 | convolution fusion | flops 1078984704 | bytes 5253120 | tf_op jit(solution)/shard_map/dot_general | solution.py:62
  62.7 4.9 %broadcast_multiply_fusion = (f32[8,64,4,128]{3,0,1,2:T(8,128)}, f32[8,64,4,128]{3,0,1,2:T(8,128)}, f32[8,64,4,128]{3,0,1,2:T(8,128)}, f32[8,64,4,128]{3,0,1,2:T(8,128)S(1)}) fusion(f32[8,64]{0,1:T(8,128)S(1)} %copy.108, f32[8,64,4,128]{3,2,1,0:T(4,128)} %reshape.273, f32[8,64,4,128]{3,2,1,0:T(4,128)} %reshape.271, f32[8,64,4,128]{3,2,1,0:T(4,128)} %reshape.272), kind=kOutput, calls=%fused_computation.64 | output fusion | flops 17563648 | bytes 7342080 | tf_op jit(solution)/shard_map/jit(cumsum)/reduce_window_sum | solution.py:112
  74.2 6.8 %convolution_multiply_fusion = f32[8,4,128,128]{3,2,1,0:T(8,128)} fusion(f32[8,64,4,128]{3,0,1,2:T(8,128)} %get-tuple-element.135, f32[8,4,128]{2,1,0:T(4,128)S(1)} %copy.107, f32[8,64,4,128]{3,2,1,0:T(4,128)} %reshape.270), kind=kOutput, calls=%fused_computation.17 | convolution fusion | flops 403177472 | bytes 4210688 | tf_op jit(solution)/shard_map/njhc,njhd->nhcd/dot_general | solution.py:124
  81.1 15.2 %while.17 = (s32[]{:T(128)}, f32[4,128,128]{2,1,0:T(8,128)S(1)}, f32[4,128]{1,0:T(4,128)S(1)}, f32[8,4,128,128]{3,2,1,0:T(8,128)}, f32[8,4,128]{2,1,0:T(4,128)S(...) while((s32[]{:T(128)}, f32[4,128,128]{2,1,0:T(8,128)S(1)}, ...), condition=%wide.region_6.7_spmd.clone, body=%wide.region_5.6_spmd.clone.sunk | while | flops 263683 | bytes 1327734 | solution.py:141
  99.3 6.4 %collective-permute-start.6 = (f32[4,128,128]{2,1,0:T(8,128)}, f32[4,128,128]{2,1,0:T(8,128)}, u32[]{:S(2)}, u32[]{:S(2)}) collective-permute-start(f32[4,128,128]{2,1,0:T(8,128)} %collective-permute-done.5), channel_id=1, source_target_pairs={{0,4},{4,8},{8,12},{12,16},{16,20},{20,24},{24,28},{28,32},{32,36}... | collective-permute-start | bytes 786440 | tf_op jit(solution)/shard_map/ppermute | solution.py:24
  105.7 3.8 %collective-permute-start = (f32[4,128]{1,0:T(4,128)S(1)}, f32[4,128]{1,0:T(4,128)S(1)}, u32[]{:S(2)}, u32[]{:S(2)}) collective-permute-start(f32[4,128]{1,0:T(4,128)S(1)} %get-tuple-element.44), channel_id=1, source_target_pairs={{0,4},{4,8},{8,12},{12,16},{16,20},{20,24},{24,28},{28,32},{32,36}... | collective-permute-start | bytes 6152 | tf_op jit(solution)/shard_map/ppermute | solution.py:18
  111.5 5.9 %collective-permute-start.7 = (f32[4,128,128]{2,1,0:T(8,128)S(1)}, f32[4,128,128]{2,1,0:T(8,128)}, u32[]{:S(2)}, u32[]{:S(2)}) collective-permute-start(f32[4,128,128]{2,1,0:T(8,128)S(1)} %add_select_fusion.4), channel_id=1, source_target_pairs={{0,8},{4,12},{8,16},{12,20},{16,24},{20,28},{24,32},{28,36},{32,40... | collective-permute-start | bytes 786440 | tf_op jit(solution)/shard_map/ppermute | solution.py:24
  119.5 5.6 %collective-permute-start.2 = (f32[4,128]{1,0:T(4,128)S(1)}, f32[4,128]{1,0:T(4,128)S(1)}, u32[]{:S(2)}, u32[]{:S(2)}) collective-permute-start(f32[4,128]{1,0:T(4,128)S(1)} %multiply_select_fusion.3), channel_id=1, source_target_pairs={{0,8},{4,12},{8,16},{12,20},{16,24},{20,28},{24,32},{28,36},{32,40... | collective-permute-start | bytes 6152 | tf_op jit(solution)/shard_map/ppermute | solution.py:23
  126.8 9.4 %collective-permute-start.8 = (f32[4,128,128]{2,1,0:T(8,128)}, f32[4,128,128]{2,1,0:T(8,128)}, u32[]{:S(2)}, u32[]{:S(2)}) collective-permute-start(f32[4,128,128]{2,1,0:T(8,128)} %add_select_fusion.3), channel_id=1, source_target_pairs={{0,16},{4,20},{8,24},{12,28},{16,32},{20,36},{24,40},{28,44},{32,4... | collective-permute-start | bytes 786440 | tf_op jit(solution)/shard_map/ppermute | solution.py:24
  140.9 5.6 %collective-permute-start.9 = (f32[4,128,128]{2,1,0:T(8,128)S(1)}, f32[4,128,128]{2,1,0:T(8,128)}, u32[]{:S(2)}, u32[]{:S(2)}) collective-permute-start(f32[4,128,128]{2,1,0:T(8,128)S(1)} %add_select_fusion.2), channel_id=1, source_target_pairs={{0,32},{4,36},{8,40},{12,44},{16,48},{20,52},{24,56},{28,60},{32,6... | collective-permute-start | bytes 786440 | tf_op jit(solution)/shard_map/ppermute | solution.py:24
  150.7 6.2 %collective-permute-start.10 = (f32[4,128,128]{2,1,0:T(8,128)S(1)}, f32[4,128,128]{2,1,0:T(8,128)S(1)}, u32[]{:S(2)}, u32[]{:S(2)}) collective-permute-start(f32[4,128,128]{2,1,0:T(8,128)S(1)} %add_select_fusion.1), channel_id=1, source_target_pairs={{0,64},{4,68},{8,72},{12,76},{16,80},{20,84},{24,88},{28,92},{32,9... | collective-permute-start | bytes 786440 | tf_op jit(solution)/shard_map/ppermute | solution.py:24
  156.9 3.6 convolution_select_fusion
  171.2 8.1 %fusion.37 = f32[512,2048]{1,0:T(8,128)} fusion(bf16[512,2048]{1,0:T(8,128)(2,1)} %param.25, f32[64,8,4,128]{3,2,1,0:T(4,128)} %bitcast.122, f32[64,8,4,128]{3,2,1,0:T(4,128)} %bitcast.124, bf16[2048,512]{1,0:T(8,128)(2,1)} %param.23, bf16[512,2048]{1,0:T(8,128)(2,1)} %all-gather.3.cloned.1.call-done, f32[2048]{0:T(1024)S(1)} %copy-done.12, ...), kind=kOutput, calls=%fused_computation.63 | convolution fusion | flops 2153512960 | bytes 12593152 | tf_op jit(solution)/shard_map/dot_general | solution.py:62
  179.3 48.6 %reduce-scatter.3.cloned.1.call-done = f32[512,512]{1,0:T(8,128)} async-done(((f32[512,2048]{1,0:T(8,128)}), f32[512,512]{1,0:T(8,128)}) %reduce-scatter.3.cloned.1.call-update) | async-done | bytes 1048592 | tf_op jit(solution)/shard_map/reduce_scatter | solution.py:70
  230.5 30.5 %all-gather.5.cloned.1.call-done = bf16[512,2048]{1,0:T(8,128)(2,1)} async-done(((bf16[512,512]{1,0:T(8,128)(2,1)}), bf16[512,2048]{1,0:T(8,128)(2,1)}) %all-gather.5.cloned.1.call-update) | async-done | bytes 2097168 | tf_op jit(solution)/shard_map/all_gather | solution.py:66
  263.3 5.0 %fusion.35 = f32[512,768]{1,0:T(8,128)} fusion(bf16[2048,768]{1,0:T(8,128)(2,1)} %param.27, bf16[512,2048]{1,0:T(8,128)(2,1)S(1)} %copy-done.6, f32[2048]{0:T(1024)S(1)} %copy-done.13, f32[512]{0:T(512)S(1)} %add_rsqrt_fusion), kind=kOutput, calls=%fused_computation.62 | convolution fusion | flops 1614807040 | bytes 6825984 | tf_op jit(solution)/shard_map/dot_general | solution.py:62
  268.3 9.0 %fusion.32 = f32[512,2048]{1,0:T(8,128)} fusion(bf16[768,2048]{1,0:T(8,128)(2,1)S(1)} %copy-done, f32[512,768]{1,0:T(8,128)} %fusion.35, bf16[2048,768]{1,0:T(8,128)(2,1)} %param.28, bf16[512,2048]{1,0:T(8,128)(2,1)} %all-gather.5.cloned.1.call-done, f32[2048]{0:T(1024)S(1)} %copy-done.13, f32[512]{0:T(512)S(1)} %add_rsqrt_fusion), kind=kOutput, calls=%fused_computation.61 | convolution fusion | flops 3227779072 | bytes 14166016 | tf_op jit(solution)/shard_map/dot_general | solution.py:62
  286.9 3.6 %constant_dynamic-slice_fusion.15 = (f32[1,64,4,128]{3,0,1,2:T(1,128)}, f32[1,64,4,128]{3,0,1,2:T(1,128)S(1)}, f32[1,64,4,128]{3,0,1,2:T(1,128)S(1)}, f32[1,64,4,128]{3,0,1,2:T(1,128)S(1)}) fusion(f32[8,64,4,128]{3,0,1,2:T(8,128)} %get-tuple-element.136, s32[]{:T(128)S(6)} %select_n.318, s32[]{:T(128)S(6)} %select_n.347, s32[]{:T(128)S(6)} %select_n.328, ...), kind=kLoop, calls=%fused_computation.123 | loop fusion | bytes 1048592 | tf_op jit(solution)/shard_map/jit(dynamic_index_in_dim)/dynamic_slice | solution.py:164
  297.1 9.1 %collective-permute-done.13 = bf16[2,4,128,128]{3,2,1,0:T(8,128)(2,1)S(1)} collective-permute-done((bf16[2,4,128,128]{3,2,1,0:T(8,128)(2,1)S(1)}, bf16[2,4,128,128]{3,2,1,0:T(8,128)(2,1)S(1)}, u32[]{:S(2)}, u32[]{:S(2)}) %collective-permute-start.13) | collective-permute-done | bytes 262176 | tf_op jit(solution)/shard_map/ppermute | solution.py:46
  306.4 11.0 %collective-permute-done.14 = bf16[2,4,128,128]{3,2,1,0:T(8,128)(2,1)S(1)} collective-permute-done((bf16[2,4,128,128]{3,2,1,0:T(8,128)(2,1)S(1)}, bf16[2,4,128,128]{3,2,1,0:T(8,128)(2,1)S(1)}, u32[]{:S(2)}, u32[]{:S(2)}) %collective-permute-start.14) | collective-permute-done | bytes 262176 | tf_op jit(solution)/shard_map/ppermute | solution.py:46
  317.5 10.8 %collective-permute-done.15 = bf16[2,4,128,128]{3,2,1,0:T(8,128)(2,1)S(1)} collective-permute-done((bf16[2,4,128,128]{3,2,1,0:T(8,128)(2,1)S(1)}, bf16[2,4,128,128]{3,2,1,0:T(8,128)(2,1)S(1)}, u32[]{:S(2)}, u32[]{:S(2)}) %collective-permute-start.15) | collective-permute-done | bytes 262176 | tf_op jit(solution)/shard_map/ppermute | solution.py:46
  331.7 7.1 %collective-permute-done.16 = bf16[2,4,128,128]{3,2,1,0:T(8,128)(2,1)} collective-permute-done((bf16[2,4,128,128]{3,2,1,0:T(8,128)(2,1)}, bf16[2,4,128,128]{3,2,1,0:T(8,128)(2,1)}, u32[]{:S(2)}, u32[]{:S(2)}) %collective-permute-start.16) | collective-permute-done | bytes 262176 | tf_op jit(solution)/shard_map/ppermute | solution.py:46
  (175 shorter events, 96.4 us)
Async XLA Ops:
  7.2 261.2 %copy-start = (bf16[768,2048]{1,0:T(8,128)(2,1)S(1)}, bf16[768,2048]{1,0:T(8,128)(2,1)}, u32[]{:S(2)}) copy-start(bf16[768,2048]{1,0:T(8,128)(2,1)} %param.29) | copy-start | bytes 9437188
  7.2 36.1 %all-gather.3.cloned.1.call-start = ((), (), s32[]{:S(2)}) async-start(), calls=%async_computation.2 | async-start | bytes 2621440 | tf_op jit(solution)/shard_map/all_gather | solution.py:66
  7.9 220.0 %reduce-scatter.3.cloned.1.call-start = ((), (), s32[]{:S(2)}) async-start(), calls=%async_computation.3 | async-start | bytes 5242880 | tf_op jit(solution)/shard_map/reduce_scatter | solution.py:70
  96.3 3.0 collective-permute-start.5
  99.3 11.0 %collective-permute-start.6 = (f32[4,128,128]{2,1,0:T(8,128)}, f32[4,128,128]{2,1,0:T(8,128)}, u32[]{:S(2)}, u32[]{:S(2)}) collective-permute-start(f32[4,128,128]{2,1,0:T(8,128)} %collective-permute-done.5), channel_id=1, source_target_pairs={{0,4},{4,8},{8,12},{12,16},{16,20},{20,24},{24,28},{28,32},{32,36}... | collective-permute-start | bytes 786440 | tf_op jit(solution)/shard_map/ppermute | solution.py:24
  105.7 4.6 %collective-permute-start = (f32[4,128]{1,0:T(4,128)S(1)}, f32[4,128]{1,0:T(4,128)S(1)}, u32[]{:S(2)}, u32[]{:S(2)}) collective-permute-start(f32[4,128]{1,0:T(4,128)S(1)} %get-tuple-element.44), channel_id=1, source_target_pairs={{0,4},{4,8},{8,12},{12,16},{16,20},{20,24},{24,28},{28,32},{32,36}... | collective-permute-start | bytes 6152 | tf_op jit(solution)/shard_map/ppermute | solution.py:18
  111.5 13.6 %collective-permute-start.7 = (f32[4,128,128]{2,1,0:T(8,128)S(1)}, f32[4,128,128]{2,1,0:T(8,128)}, u32[]{:S(2)}, u32[]{:S(2)}) collective-permute-start(f32[4,128,128]{2,1,0:T(8,128)S(1)} %add_select_fusion.4), channel_id=1, source_target_pairs={{0,8},{4,12},{8,16},{12,20},{16,24},{20,28},{24,32},{28,36},{32,40... | collective-permute-start | bytes 786440 | tf_op jit(solution)/shard_map/ppermute | solution.py:24
  117.4 2.1 collective-permute-start.1
  119.5 16.8 %collective-permute-start.2 = (f32[4,128]{1,0:T(4,128)S(1)}, f32[4,128]{1,0:T(4,128)S(1)}, u32[]{:S(2)}, u32[]{:S(2)}) collective-permute-start(f32[4,128]{1,0:T(4,128)S(1)} %multiply_select_fusion.3), channel_id=1, source_target_pairs={{0,8},{4,12},{8,16},{12,20},{16,24},{20,28},{24,32},{28,36},{32,40... | collective-permute-start | bytes 6152 | tf_op jit(solution)/shard_map/ppermute | solution.py:23
  126.8 12.9 %collective-permute-start.8 = (f32[4,128,128]{2,1,0:T(8,128)}, f32[4,128,128]{2,1,0:T(8,128)}, u32[]{:S(2)}, u32[]{:S(2)}) collective-permute-start(f32[4,128,128]{2,1,0:T(8,128)} %add_select_fusion.3), channel_id=1, source_target_pairs={{0,16},{4,20},{8,24},{12,28},{16,32},{20,36},{24,40},{28,44},{32,4... | collective-permute-start | bytes 786440 | tf_op jit(solution)/shard_map/ppermute | solution.py:24
  136.3 10.4 %collective-permute-start.3 = (f32[4,128]{1,0:T(4,128)S(1)}, f32[4,128]{1,0:T(4,128)S(1)}, u32[]{:S(2)}, u32[]{:S(2)}) collective-permute-start(f32[4,128]{1,0:T(4,128)S(1)} %multiply_select_fusion.2), channel_id=1, source_target_pairs={{0,16},{4,20},{8,24},{12,28},{16,32},{20,36},{24,40},{28,44},{32,4... | collective-permute-start | bytes 6152 | tf_op jit(solution)/shard_map/ppermute | solution.py:23
  140.9 8.8 %collective-permute-start.9 = (f32[4,128,128]{2,1,0:T(8,128)S(1)}, f32[4,128,128]{2,1,0:T(8,128)}, u32[]{:S(2)}, u32[]{:S(2)}) collective-permute-start(f32[4,128,128]{2,1,0:T(8,128)S(1)} %add_select_fusion.2), channel_id=1, source_target_pairs={{0,32},{4,36},{8,40},{12,44},{16,48},{20,52},{24,56},{28,60},{32,6... | collective-permute-start | bytes 786440 | tf_op jit(solution)/shard_map/ppermute | solution.py:24
  146.6 13.8 %collective-permute-start.4 = (f32[4,128]{1,0:T(4,128)S(1)}, f32[4,128]{1,0:T(4,128)S(1)}, u32[]{:S(2)}, u32[]{:S(2)}) collective-permute-start(f32[4,128]{1,0:T(4,128)S(1)} %multiply_select_fusion.1), channel_id=1, source_target_pairs={{0,32},{4,36},{8,40},{12,44},{16,48},{20,52},{24,56},{28,60},{32,6... | collective-permute-start | bytes 6152 | tf_op jit(solution)/shard_map/ppermute | solution.py:23
  150.7 10.0 %collective-permute-start.10 = (f32[4,128,128]{2,1,0:T(8,128)S(1)}, f32[4,128,128]{2,1,0:T(8,128)S(1)}, u32[]{:S(2)}, u32[]{:S(2)}) collective-permute-start(f32[4,128,128]{2,1,0:T(8,128)S(1)} %add_select_fusion.1), channel_id=1, source_target_pairs={{0,64},{4,68},{8,72},{12,76},{16,80},{20,84},{24,88},{28,92},{32,9... | collective-permute-start | bytes 786440 | tf_op jit(solution)/shard_map/ppermute | solution.py:24
  179.3 84.0 %copy-start.13 = (f32[2048]{0:T(1024)S(1)}, f32[2048]{0:T(1024)}, u32[]{:S(2)}) copy-start(f32[2048]{0:T(1024)} %param.26) | copy-start | bytes 24580
  179.3 81.8 %all-gather.5.cloned.1.call-start = ((), (), s32[]{:S(2)}) async-start(), calls=%async_computation.4 | async-start | bytes 2621440 | tf_op jit(solution)/shard_map/all_gather | solution.py:66
  230.3 119.6 %reduce-scatter.5.cloned.1.call-start = ((), (), s32[]{:S(2)}) async-start(), calls=%async_computation.5 | async-start | bytes 5242880 | tf_op jit(solution)/shard_map/reduce_scatter | solution.py:70
  297.0 9.2 %collective-permute-start.13 = (bf16[2,4,128,128]{3,2,1,0:T(8,128)(2,1)S(1)}, bf16[2,4,128,128]{3,2,1,0:T(8,128)(2,1)S(1)}, u32[]{:S(2)}, u32[]{:S(2)}) collective-permute-start(bf16[2,4,128,128]{3,2,1,0:T(8,128)(2,1)S(1)} %broadcast_select_fusion), channel_id=1, source_target_pairs={{0,4},{4,8},{8,12},{12,16},{16,20},{20,24},{24,28},{28,32},{32,36}... | collective-permute-start | bytes 786440 | tf_op jit(solution)/shard_map/ppermute | solution.py:46
  306.3 11.0 %collective-permute-start.14 = (bf16[2,4,128,128]{3,2,1,0:T(8,128)(2,1)S(1)}, bf16[2,4,128,128]{3,2,1,0:T(8,128)(2,1)S(1)}, u32[]{:S(2)}, u32[]{:S(2)}) collective-permute-start(bf16[2,4,128,128]{3,2,1,0:T(8,128)(2,1)S(1)} %get-tuple-element.133), channel_id=1, source_target_pairs={{0,8},{4,12},{8,16},{12,20},{16,24},{20,28},{24,32},{28,36},{32,40... | collective-permute-start | bytes 786440 | tf_op jit(solution)/shard_map/ppermute | solution.py:46
  317.4 10.9 %collective-permute-start.15 = (bf16[2,4,128,128]{3,2,1,0:T(8,128)(2,1)S(1)}, bf16[2,4,128,128]{3,2,1,0:T(8,128)(2,1)S(1)}, u32[]{:S(2)}, u32[]{:S(2)}) collective-permute-start(bf16[2,4,128,128]{3,2,1,0:T(8,128)(2,1)S(1)} %broadcast_select_fusion.2), channel_id=1, source_target_pairs={{0,16},{4,20},{8,24},{12,28},{16,32},{20,36},{24,40},{28,44},{32,4... | collective-permute-start | bytes 786440 | tf_op jit(solution)/shard_map/ppermute | solution.py:46
  329.1 9.8 %collective-permute-start.16 = (bf16[2,4,128,128]{3,2,1,0:T(8,128)(2,1)}, bf16[2,4,128,128]{3,2,1,0:T(8,128)(2,1)}, u32[]{:S(2)}, u32[]{:S(2)}) collective-permute-start(bf16[2,4,128,128]{3,2,1,0:T(8,128)(2,1)} %get-tuple-element.126), channel_id=1, source_target_pairs={{0,32},{4,36},{8,40},{12,44},{16,48},{20,52},{24,56},{28,60},{32,6... | collective-permute-start | bytes 786440 | tf_op jit(solution)/shard_map/ppermute | solution.py:46
  339.9 8.0 %collective-permute-start.17 = (bf16[2,4,128,128]{3,2,1,0:T(8,128)(2,1)S(1)}, bf16[2,4,128,128]{3,2,1,0:T(8,128)(2,1)S(1)}, u32[]{:S(2)}, u32[]{:S(2)}) collective-permute-start(bf16[2,4,128,128]{3,2,1,0:T(8,128)(2,1)S(1)} %broadcast_select_fusion.4), channel_id=1, source_target_pairs={{0,64},{4,68},{8,72},{12,76},{16,80},{20,84},{24,88},{28,92},{32,9... | collective-permute-start | bytes 786440 | tf_op jit(solution)/shard_map/ppermute | solution.py:46
  342.4 6.6 %collective-permute-start.11 = (bf16[4,128,128]{2,1,0:T(8,128)(2,1)S(1)}, bf16[4,128,128]{2,1,0:T(8,128)(2,1)S(1)}, u32[]{:S(2)}, u32[]{:S(2)}) collective-permute-start(bf16[4,128,128]{2,1,0:T(8,128)(2,1)S(1)} %fusion.15), channel_id=1, source_target_pairs={{0,124},{4,0},{8,4},{12,8},{16,12},{20,16},{24,20},{28,24},{32,28}... | collective-permute-start | bytes 393224 | tf_op jit(solution)/shard_map/ppermute | solution.py:36
  344.9 4.1 %collective-permute-start.12 = (bf16[4,128,128]{2,1,0:T(8,128)(2,1)S(1)}, bf16[4,128,128]{2,1,0:T(8,128)(2,1)S(1)}, u32[]{:S(2)}, u32[]{:S(2)}) collective-permute-start(bf16[4,128,128]{2,1,0:T(8,128)(2,1)S(1)} %fusion.16), channel_id=1, source_target_pairs={{124,60},{125,61},{126,62},{127,63}} | collective-permute-start | bytes 393224 | tf_op jit(solution)/shard_map/ppermute | solution.py:37
  (13 other events, 118.6 us)
Sparse Core Ops, SparseCore 0:
  9.7 33.5 all-gather.2
  179.4 48.5 reduce-scatter.2
  230.4 30.6 all-gather.4
  277.5 46.8 reduce-scatter.4
